TPU v7x, 128 devices: a whole 4x4x4 slice. The times are simulated.
128 devices in a mesh: row: 16 (over z, x), col: 8 (over y, core).
Axes of the slice: x: 4, y: 4, z: 4, core: 2. Of those that a mesh axis runs over, the one named last changes fastest.
Arguments:
- inputs: bfloat16 [2048, 6144], P('col', 'row'), may hold values from -6 to 6
- out_grad: bfloat16 [2048, 6144], P('col', 'row'), may hold values from -6 to 6
- pre_act: bfloat16 [2048, 24576], P('row', 'col'), may hold values from -8 to 8
- w_in: bfloat16 [6144, 24576], P('row', 'col'), may hold values from -0.078125 to 0.078125
- w_out: bfloat16 [24576, 6144], P('col', 'row'), may hold values from -0.0390625 to 0.0390625
Outputs:
- in_grad: bfloat16 [2048, 6144], P('col', 'row')
- w_in_grad: bfloat16 [6144, 24576], P('row', 'col')
- w_out_grad: bfloat16 [24576, 6144], P('col', 'row')
All inputs are finite; a program needn't handle non-finite values.
Results may differ from a plain program's by a relative error of at most 0.03.
Values may be sent and summed in bfloat16 or wider, within the bound.
No kernel may reach another device: no remote copies, remote signals or barrier semaphores. Data moves between devices by JAX's collectives and lax.ppermute only.
A program may use at most 128 MiB of HBM per device.

v0:
```python
import jax
import jax.numpy as jnp
from jax import lax
from jax.sharding import PartitionSpec as P


def gelu_parts(pre_act):
    value = pre_act.astype(jnp.float32)
    cumul = 0.5 * (1.0 + jax.scipy.special.erf(value * 0.7071067811865476))
    density = jnp.exp(-0.5 * value * value) * 0.3989422804014327
    return (value * cumul, cumul + value * density)


def on_device(inputs, out_grad, pre_act, w_in, w_out):
    inputs_all, grad_all = (
        lax.all_gather(inputs, "col", axis=0, tiled=True),
        lax.all_gather(out_grad, "col", axis=0, tiled=True),
    )
    block = grad_all
    total = lax.psum(
        lax.dot_general(
            block, w_out, (((1,), (1,)), ((), ())), preferred_element_type=jnp.float32
        ).astype(jnp.bfloat16),
        "row",
    ).astype(jnp.float32)
    pre_all = lax.all_gather(pre_act, "row", axis=0, tiled=True)
    value, slope = gelu_parts(pre_all)
    hidden = value.astype(jnp.bfloat16)
    pre_grad = (total * slope).astype(jnp.bfloat16)
    w_out_grad = lax.dot_general(
        hidden, grad_all, (((0,), (0,)), ((), ())), preferred_element_type=jnp.float32
    ).astype(jnp.bfloat16)
    w_in_grad = lax.dot_general(
        inputs_all, pre_grad, (((0,), (0,)), ((), ())), preferred_element_type=jnp.float32
    ).astype(jnp.bfloat16)
    block = pre_grad
    in_grad = lax.psum_scatter(
        lax.dot_general(
            block, w_in, (((1,), (1,)), ((), ())), preferred_element_type=jnp.float32
        ).astype(jnp.bfloat16),
        "col",
        scatter_dimension=0,
        tiled=True,
    )
    return (in_grad, w_in_grad, w_out_grad)


def solution(mesh):
    in_specs = (P("col", "row"), P("col", "row"), P("row", "col"), P("row", "col"), P("col", "row"))
    out_specs = (P("col", "row"), P("row", "col"), P("col", "row"))
    return jax.shard_map(
        on_device, mesh=mesh, in_specs=in_specs, out_specs=out_specs, check_vma=False
    )
```

profile of v0, /device:TPU:0, one launch (start us, length us, event | category | flops | bytes accessed | tf_op | source)
XLA Modules:
  0.0 386.3 jit_solution(935208402461848215)
XLA Ops:
  7.2 0.0 copy-start
  7.2 0.0 all-gather.4.cloned.1.call-start
  7.2 0.7 all-gather.4.cloned.1.call-update
  7.9 0.0 all-reduce.2.cloned.1.call-start
  8.0 28.5 %all-gather.4.cloned.1.call-done = bf16[2048,384]{1,0:T(8,128)(2,1)} async-done(((bf16[256,384]{1,0:T(8,128)(2,1)}), bf16[2048,384]{1,0:T(8,128)(2,1)}) %all-gather.4.cloned.1.call-update) | async-done | bytes 1572880 | tf_op jit(solution)/shard_map/all_gather | solution.py:17
  36.5 0.0 copy-done
  36.5 11.2 %convolution_convert_fusion = bf16[2048,3072]{1,0:T(8,128)(2,1)} fusion(bf16[2048,384]{1,0:T(8,128)(2,1)} %all-gather.4.cloned.1.call-done, bf16[3072,384]{1,0:T(8,128)(2,1)S(1)} %copy-done), kind=kOutput, calls=%fused_computation.15 | convolution fusion | flops 4838129664 | bytes 16515072 | tf_op jit(solution)/shard_map/dot_general | solution.py:21
  47.6 0.0 all-reduce.2.cloned.1.call-update
  47.7 0.0 all-gather.6.cloned.1.call-start
  47.7 0.7 all-gather.6.cloned.1.call-update
  48.4 0.0 all-gather.8.cloned.1.call-start
  48.5 0.5 all-gather.8.cloned.1.call-update
  49.0 0.0 copy-start.3
  49.0 0.0 reduce-scatter.2.cloned.1.call-start
  49.0 177.4 %all-reduce.2.cloned.1.call-done = bf16[2048,3072]{1,0:T(8,128)(2,1)} async-done(((bf16[2048,3072]{1,0:T(8,128)(2,1)}), bf16[2048,3072]{1,0:T(8,128)(2,1)}) %all-reduce.2.cloned.1.call-update) | async-done | bytes 12582928 | tf_op jit(solution)/shard_map/psum | solution.py:20
  226.4 91.8 %all-gather.6.cloned.1.call-done = bf16[2048,3072]{1,0:T(8,128)(2,1)} async-done(((bf16[128,3072]{1,0:T(8,128)(2,1)}), bf16[2048,3072]{1,0:T(8,128)(2,1)}) %all-gather.6.cloned.1.call-update) | async-done | bytes 12582928 | tf_op jit(solution)/shard_map/all_gather | solution.py:26
  318.2 13.7 %fusion.7 = bf16[2048,3072]{1,0:T(8,128)(2,1)S(1)} fusion(bf16[2048,3072]{1,0:T(8,128)(2,1)} %all-gather.6.cloned.1.call-done, bf16[2048,3072]{1,0:T(8,128)(2,1)} %all-reduce.2.cloned.1.call-done), kind=kLoop, calls=%fused_computation.12 | loop fusion | flops 75497472 | bytes 37748736 | tf_op jit(solution)/shard_map/convert_element_type | solution.py:29
  331.9 0.0 copy-start.2
  331.9 4.5 %copy-done.2 = bf16[2048,3072]{1,0:T(8,128)(2,1)} copy-done((bf16[2048,3072]{1,0:T(8,128)(2,1)}, bf16[2048,3072]{1,0:T(8,128)(2,1)S(1)}, u32[]{:S(2)}) %copy-start.2) | copy-done | bytes 12582936
  336.4 0.0 copy-done.3
  336.4 7.8 %convolution_convert_fusion.2 = bf16[2048,384]{1,0:T(8,128)(2,1)} fusion(bf16[2048,3072]{1,0:T(8,128)(2,1)S(1)} %fusion.7, bf16[384,3072]{1,0:T(8,128)(2,1)S(1)} %copy-done.3), kind=kOutput, calls=%fused_computation.19 | convolution fusion | flops 4832624640 | bytes 16515072 | tf_op jit(solution)/shard_map/dot_general | solution.py:38
  344.2 0.0 reduce-scatter.2.cloned.1.call-update
  344.2 0.0 all-gather.8.cloned.1.call-done
  344.2 10.2 %fusion.14 = bf16[384,3072]{0,1:T(8,128)(2,1)S(1)} fusion(bf16[2048,3072]{1,0:T(8,128)(2,1)} %copy-done.2, bf16[2048,384]{1,0:T(8,128)(2,1)} %all-gather.8.cloned.1.call-done), kind=kOutput, calls=%fused_computation.18 | convolution fusion | flops 4833017856 | bytes 16515072 | tf_op jit(solution)/shard_map/dot_general | solution.py:33
  354.4 2.6 copy.8
  357.0 0.0 copy-start.1
  357.0 11.9 %fusion.11 = bf16[3072,384]{1,0:T(8,128)(2,1)} fusion(bf16[2048,384]{1,0:T(8,128)(2,1)} %all-gather.4.cloned.1.call-done, bf16[2048,3072]{1,0:T(8,128)(2,1)} %all-gather.6.cloned.1.call-done), kind=kOutput, calls=%fused_computation.16 | convolution fusion | flops 4870766592 | bytes 16515072 | tf_op jit(solution)/shard_map/dot_general | solution.py:30
  368.9 10.8 %reduce-scatter.2.cloned.1.call-done = bf16[256,384]{1,0:T(8,128)(2,1)} async-done(((bf16[2048,384]{1,0:T(8,128)(2,1)}), bf16[256,384]{1,0:T(8,128)(2,1)}) %reduce-scatter.2.cloned.1.call-update) | async-done | bytes 196624 | tf_op jit(solution)/shard_map/reduce_scatter | solution.py:37
  379.7 0.0 copy-done.1
Async XLA Ops:
  7.2 29.3 %copy-start = (bf16[3072,384]{1,0:T(8,128)(2,1)S(1)}, bf16[3072,384]{1,0:T(8,128)(2,1)}, u32[]{:S(2)}) copy-start(bf16[3072,384]{1,0:T(8,128)(2,1)} %param.9) | copy-start | bytes 7077892
  7.2 29.3 %all-gather.4.cloned.1.call-start = ((), (), s32[]{:S(2)}) async-start(), calls=%async_computation.1 | async-start | bytes 1769472 | tf_op jit(solution)/shard_map/all_gather | solution.py:17
  7.9 218.5 %all-reduce.2.cloned.1.call-start = ((), (), s32[]{:S(2)}) async-start(), calls=%async_computation.2 | async-start | bytes 25165824 | tf_op jit(solution)/shard_map/psum | solution.py:20
  47.7 270.5 %all-gather.6.cloned.1.call-start = ((), (), s32[]{:S(2)}) async-start(), calls=%async_computation.3 | async-start | bytes 13369344 | tf_op jit(solution)/shard_map/all_gather | solution.py:26
  48.4 295.8 %all-gather.8.cloned.1.call-start = ((), (), s32[]{:S(2)}) async-start(), calls=%async_computation.5 | async-start | bytes 1769472 | tf_op jit(solution)/shard_map/all_gather | solution.py:16
  49.0 287.4 %copy-start.3 = (bf16[384,3072]{1,0:T(8,128)(2,1)S(1)}, bf16[384,3072]{1,0:T(8,128)(2,1)}, u32[]{:S(2)}) copy-start(bf16[384,3072]{1,0:T(8,128)(2,1)} %param.8) | copy-start | bytes 7077892
  49.0 330.7 %reduce-scatter.2.cloned.1.call-start = ((), (), s32[]{:S(2)}) async-start(), calls=%async_computation.4 | async-start | bytes 1769472 | tf_op jit(solution)/shard_map/reduce_scatter | solution.py:37
  331.9 4.5 %copy-start.2 = (bf16[2048,3072]{1,0:T(8,128)(2,1)}, bf16[2048,3072]{1,0:T(8,128)(2,1)S(1)}, u32[]{:S(2)}) copy-start(bf16[2048,3072]{1,0:T(8,128)(2,1)S(1)} %fusion.7) | copy-start | bytes 37748740
  357.0 22.7 %copy-start.1 = (bf16[3072,384]{1,0:T(8,128)(2,1)S(1)}, bf16[3072,384]{1,0:T(8,128)(2,1)}, u32[]{:S(2)}) copy-start(bf16[3072,384]{1,0:T(8,128)(2,1)} %param.9) | copy-start | bytes 7077892
Sparse Core Ops, SparseCore 0:
  9.7 26.7 all-gather.3
  47.8 178.6 all-reduce.1
  228.6 89.5 all-gather.5
  319.8 23.8 all-gather.7
  346.5 33.1 reduce-scatter.1
where the time goes:
time: 387 us; the launch traced here: 386 us
  waiting for transfers between devices  310 us (80%)
  matrix products  41 us (11%)
  between operations  13.8 us (4%)
  other arithmetic  13.7 us (4%)
  local copies, waits for them, and re-layouts  7.09 us (2%)
    psum x1, waiting for transfers between devices, on_device(): lax.psum(lax.dot_general(block, w_out, (((1,), (1,)), ((), ())), preferre...  177 us
    all_gather x1, waiting for transfers between devices, on_device(): pre_all = lax.all_gather(pre_act, 'row', axis=0, tiled=True)  91.8 us
    all_gather x1, waiting for transfers between devices, on_device(): lax.all_gather(out_grad, 'col', axis=0, tiled=True)  28.5 us
    convert_element_type x1, other arithmetic, on_device(): pre_grad = (total * slope).astype(jnp.bfloat16)  13.7 us
    dot_general x1, matrix products, on_device(): lax.dot_general(hidden, grad_all, (((0,), (0,)), ((), ())), preferred_ele...  11.9 us
    dot_general x1, matrix products, on_device(): lax.dot_general(block, w_out, (((1,), (1,)), ((), ())), preferred_element...  11.2 us
    reduce_scatter x1, waiting for transfers between devices, on_device(): lax.psum_scatter(lax.dot_general(block, w_in, (((1,), (1,)), ((), ())), p...  10.8 us
    dot_general x1, matrix products, on_device(): lax.dot_general(inputs_all, pre_grad, (((0,), (0,)), ((), ())), preferred...  10.2 us
  transfers between devices with their start and end apart: 5, of which 4 were waited for; matrix products, arithmetic and copies ran while one was open for 12% of the time, Pallas kernels for 0%

commit v1 on v0

--- a/solution.py
+++ b/solution.py
@@ -2,6 +2,14 @@
 import jax.numpy as jnp
 from jax import lax
 from jax.sharding import PartitionSpec as P
+
+
+def gather_from_all(shard, axis, dim):
+    length = lax.axis_size(axis)
+    repeats = [length if d == dim else 1 for d in range(shard.ndim)]
+    return lax.all_to_all(
+        jnp.tile(shard, repeats), axis, split_axis=dim, concat_axis=dim, tiled=True
+    )
 
 
 def gelu_parts(pre_act):
@@ -23,7 +31,7 @@
         ).astype(jnp.bfloat16),
         "row",
     ).astype(jnp.float32)
-    pre_all = lax.all_gather(pre_act, "row", axis=0, tiled=True)
+    pre_all = gather_from_all(pre_act, "row", 0)
     value, slope = gelu_parts(pre_all)
     hidden = value.astype(jnp.bfloat16)
     pre_grad = (total * slope).astype(jnp.bfloat16)

time: 387 us -> 463 us (1.20)
  waiting for transfers between devices: 310 us -> 361 us
  local copies, waits for them, and re-layouts: 7.09 us -> 14.3 us
  starting transfers between devices: 0.19 us -> 7.32 us
  matrix products: 41 us -> 46.6 us
  other arithmetic: 13.7 us -> 19.3 us
    all_to_all x0 -> x1, waiting for transfers between devices: none -> 217 us  [gather_from_all(): lax.all_to_all(jnp.tile(shard, repeats), axis, split_axis=dim, concat_axi...]
    all_gather x1 -> x0, waiting for transfers between devices: 91.8 us -> none  [on_device(): pre_all = lax.all_gather(pre_act, 'row', axis=0, tiled=True)]
    psum x1, waiting for transfers between devices: 177 us -> 112 us  [on_device(): lax.psum(lax.dot_general(block, w_out, (((1,), (1,)), ((), ())), preferre...]
    reduce_scatter x1, waiting for transfers between devices: 10.8 us -> 2.39 us  [on_device(): lax.psum_scatter(lax.dot_general(block, w_in, (((1,), (1,)), ((), ())), p...]
    all_to_all x0 -> x1, starting transfers between devices: none -> 6.99 us  [gather_from_all(): lax.all_to_all(jnp.tile(shard, repeats), axis, split_axis=dim, concat_axi...]
    another operation x0 -> x1, local copies, waits for them, and re-layouts: none -> 6.07 us  [gather_from_all(): jnp.tile(shard, repeats)]
    dot_general x1, matrix products: 11.9 us -> 17.6 us  [on_device(): lax.dot_general(hidden, grad_all, (((0,), (0,)), ((), ())), preferred_ele...]
    convert_element_type x1, other arithmetic: 13.7 us -> 19.3 us  [on_device(): pre_grad = (total * slope).astype(jnp.bfloat16)]
  transfers between devices with their start and end apart: 5 -> 5, of which waited for: 4 -> 4; matrix products, arithmetic and copies ran while one was open for 12% -> 14% of each run, Pallas kernels for 0% -> 0%
where the time goes in v1:
time: 463 us
  waiting for transfers between devices  361 us (78%)
  matrix products  46.6 us (10%)
  other arithmetic  19.3 us (4%)
  local copies, waits for them, and re-layouts  14.3 us (3%)
  between operations  13.8 us (3%)
  starting transfers between devices  7.32 us (2%)
    all_to_all x1, waiting for transfers between devices, gather_from_all(): lax.all_to_all(jnp.tile(shard, repeats), axis, split_axis=dim, concat_axi...  217 us
    psum x1, waiting for transfers between devices, on_device(): lax.psum(lax.dot_general(block, w_out, (((1,), (1,)), ((), ())), preferre...  112 us
    all_gather x1, waiting for transfers between devices, on_device(): lax.all_gather(out_grad, 'col', axis=0, tiled=True)  28.5 us
    convert_element_type x1, other arithmetic, on_device(): pre_grad = (total * slope).astype(jnp.bfloat16)  19.3 us
    dot_general x1, matrix products, on_device(): lax.dot_general(hidden, grad_all, (((0,), (0,)), ((), ())), preferred_ele...  17.6 us
    dot_general x1, matrix products, on_device(): lax.dot_general(block, w_out, (((1,), (1,)), ((), ())), preferred_element...  11.1 us
    dot_general x1, matrix products, on_device(): lax.dot_general(inputs_all, pre_grad, (((0,), (0,)), ((), ())), preferred...  10.2 us
  transfers between devices with their start and end apart: 5, of which 4 were waited for; matrix products, arithmetic and copies ran while one was open for 14% of the time, Pallas kernels for 0%

profile of v1, /device:TPU:0, one launch (start us, length us, event | category | flops | bytes accessed | tf_op | source)
XLA Modules:
  0.0 462.7 jit_solution(16991427651168239457)
XLA Ops:
  7.2 0.0 copy-start
  7.2 0.0 all-gather.3.cloned.1.call-start
  7.2 0.7 all-gather.3.cloned.1.call-update
  7.9 0.0 all-reduce.2.cloned.1.call-start
  8.0 28.5 %all-gather.3.cloned.1.call-done = bf16[2048,384]{1,0:T(8,128)(2,1)} async-done(((bf16[256,384]{1,0:T(8,128)(2,1)}), bf16[2048,384]{1,0:T(8,128)(2,1)}) %all-gather.3.cloned.1.call-update) | async-done | bytes 1572880 | tf_op jit(solution)/shard_map/all_gather | solution.py:25
  36.5 0.0 copy-done
  36.5 11.1 %convolution_convert_fusion = bf16[2048,3072]{1,0:T(8,128)(2,1)} fusion(bf16[2048,384]{1,0:T(8,128)(2,1)} %all-gather.3.cloned.1.call-done, bf16[3072,384]{1,0:T(8,128)(2,1)S(1)} %copy-done), kind=kOutput, calls=%fused_computation.15 | convolution fusion | flops 4838129664 | bytes 16515072 | tf_op jit(solution)/shard_map/dot_general | solution.py:29
  47.6 0.0 copy-start.3
  47.6 0.0 all-reduce.2.cloned.1.call-update
  47.6 1.1 copy-done.3
  48.7 6.1 %tile.2 = bf16[16,128,3072]{2,1,0:T(8,128)(2,1)} broadcast(bf16[128,3072]{1,0:T(8,128)(2,1)S(1)} %copy-done.3), dimensions={1,2} | broadcast | bytes 13369344 | tf_op jit(solution)/shard_map/tile | solution.py:11
  54.8 7.0 %all-to-all-start = ((bf16[16,128,3072]{2,1,0:T(8,128)(2,1)}), bf16[16,128,3072]{2,1,0:T(8,128)(2,1)}, u32[]{:S(2)}, u32[]{:S(2)}) async-start(bf16[16,128,3072]{2,1,0:T(8,128)(2,1)} %tile.2), calls=%async_computation | async-start | bytes 25165824 | tf_op jit(solution)/shard_map/all_to_all | solution.py:10
  61.8 0.0 all-gather.5.cloned.1.call-start
  61.8 0.7 all-gather.5.cloned.1.call-update
  62.5 0.0 copy-start.4
  62.5 0.2 reduce-scatter.2.cloned.1.call-start
  62.8 216.9 %all-to-all-done = bf16[16,128,3072]{2,1,0:T(8,128)(2,1)} async-done(((bf16[16,128,3072]{2,1,0:T(8,128)(2,1)}), bf16[16,128,3072]{2,1,0:T(8,128)(2,1)}, u32[]{:S(2)}, u32[]{:S(2)}) %all-to-all-start) | async-done | bytes 12582944 | tf_op jit(solution)/shard_map/all_to_all | solution.py:10
  279.7 112.1 %all-reduce.2.cloned.1.call-done = bf16[2048,3072]{1,0:T(8,128)(2,1)} async-done(((bf16[2048,3072]{1,0:T(8,128)(2,1)}), bf16[2048,3072]{1,0:T(8,128)(2,1)}) %all-reduce.2.cloned.1.call-update) | async-done | bytes 12582928 | tf_op jit(solution)/shard_map/psum | solution.py:28
  391.8 19.3 %fusion.7 = (bf16[2048,3072]{1,0:T(8,128)(2,1)S(1)}, f32[2048,3072]{1,0:T(8,128)}) fusion(bf16[2048,3072]{1,0:T(8,128)(2,1)} %all-reduce.2.cloned.1.call-done, bf16[16,128,3072]{2,1,0:T(8,128)(2,1)} %all-to-all-done), kind=kLoop, calls=%fused_computation.12 | loop fusion | flops 75497472 | bytes 62914560 | tf_op jit(solution)/shard_map/convert_element_type | solution.py:37
  411.0 0.0 copy-start.2
  411.0 4.5 copy-done.2
  415.5 0.0 copy-done.4
  415.5 7.8 %convolution_convert_fusion.2 = bf16[2048,384]{1,0:T(8,128)(2,1)} fusion(bf16[2048,3072]{1,0:T(8,128)(2,1)S(1)} %get-tuple-element.6, bf16[384,3072]{1,0:T(8,128)(2,1)S(1)} %copy-done.4), kind=kOutput, calls=%fused_computation.19 | convolution fusion | flops 4832624640 | bytes 16515072 | tf_op jit(solution)/shard_map/dot_general | solution.py:46
  423.3 0.0 reduce-scatter.2.cloned.1.call-update
  423.3 0.0 all-gather.5.cloned.1.call-done
  423.3 10.2 %fusion.14 = bf16[384,3072]{0,1:T(8,128)(2,1)S(1)} fusion(bf16[2048,3072]{1,0:T(8,128)(2,1)} %copy-done.2, bf16[2048,384]{1,0:T(8,128)(2,1)} %all-gather.5.cloned.1.call-done), kind=kOutput, calls=%fused_computation.18 | convolution fusion | flops 4833017856 | bytes 16515072 | tf_op jit(solution)/shard_map/dot_general | solution.py:41
  433.5 2.6 copy.8
  436.1 0.0 copy-start.1
  436.1 17.6 %fusion.11 = bf16[3072,384]{1,0:T(8,128)(2,1)} fusion(bf16[2048,384]{1,0:T(8,128)(2,1)} %all-gather.3.cloned.1.call-done, f32[2048,3072]{1,0:T(8,128)} %get-tuple-element.7, bf16[2048,3072]{1,0:T(8,128)(2,1)} %bitcast.1), kind=kOutput, calls=%fused_computation.16 | convolution fusion | flops 4851892224 | bytes 41680896 | tf_op jit(solution)/shard_map/dot_general | solution.py:38
  453.7 2.4 reduce-scatter.2.cloned.1.call-done
  456.1 0.0 copy-done.1
Async XLA Ops:
  7.2 29.3 %copy-start = (bf16[3072,384]{1,0:T(8,128)(2,1)S(1)}, bf16[3072,384]{1,0:T(8,128)(2,1)}, u32[]{:S(2)}) copy-start(bf16[3072,384]{1,0:T(8,128)(2,1)} %param.9) | copy-start | bytes 7077892
  7.2 29.3 %all-gather.3.cloned.1.call-start = ((), (), s32[]{:S(2)}) async-start(), calls=%async_computation.2 | async-start | bytes 1769472 | tf_op jit(solution)/shard_map/all_gather | solution.py:25
  7.9 383.9 %all-reduce.2.cloned.1.call-start = ((), (), s32[]{:S(2)}) async-start(), calls=%async_computation.3 | async-start | bytes 25165824 | tf_op jit(solution)/shard_map/psum | solution.py:28
  47.6 1.1 copy-start.3
  54.8 224.9 %all-to-all-start = ((bf16[16,128,3072]{2,1,0:T(8,128)(2,1)}), bf16[16,128,3072]{2,1,0:T(8,128)(2,1)}, u32[]{:S(2)}, u32[]{:S(2)}) async-start(bf16[16,128,3072]{2,1,0:T(8,128)(2,1)} %tile.2), calls=%async_computation | async-start | bytes 25165824 | tf_op jit(solution)/shard_map/all_to_all | solution.py:10
  61.8 361.5 %all-gather.5.cloned.1.call-start = ((), (), s32[]{:S(2)}) async-start(), calls=%async_computation.5 | async-start | bytes 1769472 | tf_op jit(solution)/shard_map/all_gather | solution.py:24
  62.5 353.0 %copy-start.4 = (bf16[384,3072]{1,0:T(8,128)(2,1)S(1)}, bf16[384,3072]{1,0:T(8,128)(2,1)}, u32[]{:S(2)}) copy-start(bf16[384,3072]{1,0:T(8,128)(2,1)} %param.8) | copy-start | bytes 7077892
  62.5 393.6 %reduce-scatter.2.cloned.1.call-start = ((), (), s32[]{:S(2)}) async-start(), calls=%async_computation.4 | async-start | bytes 1769472 | tf_op jit(solution)/shard_map/reduce_scatter | solution.py:45
  411.0 4.5 copy-start.2
  436.1 20.0 %copy-start.1 = (bf16[3072,384]{1,0:T(8,128)(2,1)S(1)}, bf16[3072,384]{1,0:T(8,128)(2,1)}, u32[]{:S(2)}) copy-start(bf16[3072,384]{1,0:T(8,128)(2,1)} %param.9) | copy-start | bytes 7077892
Sparse Core Ops, SparseCore 0:
  9.7 26.7 all-gather.2
  47.7 344.0 all-reduce.1
  393.5 23.9 all-gather.4
  423.4 32.6 reduce-scatter.1
